TPU v7x, 32 devices: a whole 2x2x4 slice. The times are simulated.
32 devices in a mesh: expert: 8 (over z, y), shard: 4 (over x, core).
Axes of the slice: x: 2, y: 2, z: 4, core: 2. Of those that a mesh axis runs over, the one named last changes fastest.
Arguments:
- tokens: float32 [25216, 512], P(('expert', 'shard')), may hold values from -6 to 6
- routes: int32 [25216, 2], P(('expert', 'shard')), may hold values from 0 to 7, all different within a row; in each aligned block of 394 rows (0 to 393, 394 to 787, ...) at most 192 rows name the same one
- priority: int32 [25216], P(('expert', 'shard')), may hold values from 0 to 393, as said below
- norm_gain: bfloat16 [2, 2, 512], P(None, None, 'shard'), may hold values from 0.5 to 1.5
- norm_bias: bfloat16 [2, 2, 512], P(None, None, 'shard'), may hold values from -1 to 1
- w_qkv: bfloat16 [2, 512, 1536], P(None, 'shard'), may hold values from -0.25 to 0.25
- w_proj: bfloat16 [2, 512, 512], P(None, 'shard'), may hold values from -2 to 2
- w_router: bfloat16 [2, 512, 8], P(None, 'shard'), may hold values from -0.1875 to 0.1875
- exp_in: bfloat16 [2, 8, 512, 2048], P(None, 'expert', 'shard'), may hold values from -0.25 to 0.25
- exp_out: bfloat16 [2, 8, 2048, 512], P(None, 'expert', 'shard'), may hold values from -0.875 to 0.875
- cotangent: float32 [25216, 512], P(('expert', 'shard')), may hold values from -6 to 6
Outputs:
- activations: float32 [25216, 512], P(('expert', 'shard'))
- d_tokens: float32 [25216, 512], P(('expert', 'shard'))
- grad_gain: float32 [2, 2, 512], P(None, None, 'shard')
- grad_bias: float32 [2, 2, 512], P(None, None, 'shard')
- grad_qkv: float32 [2, 512, 1536], P(None, 'shard')
- grad_proj: float32 [2, 512, 512], P(None, 'shard')
- grad_router: float32 [2, 512, 8], P(None, 'shard')
- grad_exp_in: float32 [2, 8, 512, 2048], P(None, 'expert', 'shard')
- grad_exp_out: float32 [2, 8, 2048, 512], P(None, 'expert', 'shard')
Inputs may be any that keep to these rules, and one draw needn't show every extreme that they name: `routes`: each row names 2 different experts; in each aligned block of 394 rows no expert is named by more than 192 rows. `priority`: in each aligned block of 394 rows the values are a permutation of 0 to 393.
All inputs are finite; a program needn't handle non-finite values.
Results may differ from a plain program's by a relative error of at most 0.025.
Values may be sent and summed in bfloat16 or wider, within the bound.
No kernel may reach another device: no remote copies, remote signals or barrier semaphores. Data moves between devices by JAX's collectives and lax.ppermute only.
A program may use at most 256 MiB of HBM per device.

v0:
```python
import jax
import jax.numpy as jnp
from jax import lax
from jax.sharding import PartitionSpec as P

D = 512
HEADS = 8
HEAD = 64
HIDDEN_SIZE = 2048
EXP_DEV = 1
SEQ = 197
MICRO = 2
LAYERS = 2
TOP = 2
TOK_MB = 394
norm_eps = 1e-06


def layer_norm(values, norm_scale, norm_shift):
    centre = values - jnp.mean(values, axis=-1, keepdims=True)
    spread = jnp.mean(centre * centre, axis=-1, keepdims=True)
    return centre * lax.rsqrt(spread + norm_eps) * norm_scale + norm_shift


def gelu_tanh(values):
    return jax.nn.gelu(values, approximate=True)


def dot_first(left, right):
    return lax.dot_general(
        left, right, (((0,), (0,)), ((), ())), preferred_element_type=jnp.float32
    )


def dot_last(left, right):
    return lax.dot_general(
        left, right, (((1,), (1,)), ((), ())), preferred_element_type=jnp.float32
    )


def slot_tables(route_ids, prio_rank, experts, capacity):
    tok_count = route_ids.shape[0]
    order_key = jnp.concatenate([prio_rank, prio_rank + tok_count])
    pair_expert = jnp.concatenate([route_ids[:, 0], route_ids[:, 1]])
    same_expert = pair_expert[:, None] == pair_expert[None, :]
    earlier = order_key[None, :] < order_key[:, None]
    position = jnp.sum((same_expert & earlier).astype(jnp.int32), axis=1)
    kept_mask = position < capacity
    flat_slot = jnp.where(kept_mask, pair_expert * capacity + position, experts * capacity)
    pair_ids = jnp.arange(2 * tok_count, dtype=jnp.int32)
    slot_pair = (
        jnp.full((experts * capacity + 1,), 2 * tok_count, jnp.int32).at[flat_slot].set(pair_ids)
    )
    slot_pair = slot_pair[: experts * capacity]
    slot_token = jnp.where(slot_pair < 2 * tok_count, slot_pair % tok_count, tok_count)
    return (flat_slot, slot_pair, slot_token, kept_mask)


def forward_layer(residual, route_ids, prio_rank, weights, experts, capacity):
    norm_gains, norm_shifts, qkv_w, proj_w, router_w, in_w, out_w = weights
    tok_count = residual.shape[0]
    seq_count = tok_count // SEQ
    score_scale = HEAD ** (-0.5)
    norm_scale = norm_gains.astype(jnp.float32)
    norm_shift = norm_shifts.astype(jnp.float32)
    normed = layer_norm(residual, norm_scale[0], norm_shift[0]).astype(jnp.bfloat16)
    qkv_rows = jnp.dot(normed, qkv_w, preferred_element_type=jnp.float32).astype(jnp.bfloat16)
    heads = qkv_rows.reshape(seq_count, SEQ, 3, HEADS, HEAD)
    scores = (
        jnp.einsum(
            "sqhd,skhd->shqk", heads[:, :, 0], heads[:, :, 1], preferred_element_type=jnp.float32
        )
        * score_scale
    )
    row_top = jnp.max(scores, axis=-1, keepdims=True)
    scores_exp = jnp.exp(scores - row_top)
    row_total = jnp.sum(scores_exp, axis=-1, keepdims=True)
    soft_scores = scores_exp / row_total
    log_total = row_top + jnp.log(row_total)
    mixed_heads = jnp.einsum(
        "shqk,skhd->sqhd",
        soft_scores.astype(jnp.bfloat16),
        heads[:, :, 2],
        preferred_element_type=jnp.float32,
    )
    mixed_heads = mixed_heads.astype(jnp.bfloat16).reshape(tok_count, D)
    middle = residual + jnp.dot(mixed_heads, proj_w, preferred_element_type=jnp.float32)
    normed_two = layer_norm(middle, norm_scale[1], norm_shift[1]).astype(jnp.bfloat16)
    gate_probs = jax.nn.softmax(
        jnp.dot(normed_two, router_w, preferred_element_type=jnp.float32), axis=-1
    )
    flat_slot, slot_pair, slot_token, kept_mask = slot_tables(
        route_ids, prio_rank, experts, capacity
    )
    padded = jnp.concatenate([normed_two, jnp.zeros((1, D), jnp.bfloat16)])
    sending = padded[slot_token].reshape(experts, capacity, D)
    received = lax.all_to_all(sending, "expert", split_axis=0, concat_axis=0, tiled=True)
    sources = received.shape[0]
    item_count = received.shape[1]
    row_block = received.reshape(sources * item_count, D)
    hidden_pre = jnp.dot(row_block, in_w[0], preferred_element_type=jnp.float32)
    hidden_act = gelu_tanh(hidden_pre).astype(jnp.bfloat16)
    expert_rows = jnp.dot(hidden_act, out_w[0], preferred_element_type=jnp.float32).astype(
        jnp.bfloat16
    )
    returned = lax.all_to_all(
        expert_rows.reshape(sources, item_count, D),
        "expert",
        split_axis=0,
        concat_axis=0,
        tiled=True,
    )
    returned, received, hidden_pre = (
        returned,
        received,
        hidden_pre.reshape(sources, item_count, HIDDEN_SIZE),
    )
    back_rows = jnp.concatenate(
        [returned.reshape(experts * capacity, D), jnp.zeros((1, D), jnp.bfloat16)]
    )
    pair_rows = back_rows[flat_slot].astype(jnp.float32).reshape(TOP, tok_count, D)
    route_hot = (
        route_ids[:, :, None] == jnp.arange(experts, dtype=jnp.int32)[None, None, :]
    ).astype(jnp.float32)
    chosen = jnp.sum(route_hot * gate_probs[:, None, :], axis=-1)
    kept_gate = kept_mask.astype(jnp.float32).reshape(TOP, tok_count)
    weight_pair = kept_gate * chosen.T
    combined = jnp.sum(weight_pair[:, :, None] * pair_rows, axis=0)
    output = middle + combined
    saved_state = (
        residual,
        normed,
        heads,
        log_total,
        mixed_heads,
        middle,
        normed_two,
        gate_probs,
        route_hot,
        kept_gate,
        weight_pair,
        flat_slot,
        slot_pair,
        pair_rows,
        received,
        hidden_pre,
    )
    return (output, saved_state)


def backward_layer(d_output, saved_state, weights, experts, capacity):
    (
        residual,
        normed,
        heads,
        log_total,
        mixed_heads,
        middle,
        normed_two,
        gate_probs,
        route_hot,
        kept_gate,
        weight_pair,
        flat_slot,
        slot_pair,
        pair_rows,
        received,
        hidden_pre,
    ) = saved_state
    norm_gains, norm_shifts, qkv_w, proj_w, router_w, in_w, out_w = weights
    tok_count = residual.shape[0]
    seq_count = tok_count // SEQ
    score_scale = HEAD ** (-0.5)
    norm_scale = norm_gains.astype(jnp.float32)
    norm_shift = norm_shifts.astype(jnp.float32)
    d_gate_pair = kept_gate * jnp.sum(d_output[None] * pair_rows, axis=-1)
    d_gates = jnp.sum(route_hot * d_gate_pair.T[:, :, None], axis=1)
    d_logits = (
        gate_probs * (d_gates - jnp.sum(gate_probs * d_gates, axis=-1, keepdims=True))
    ).astype(jnp.bfloat16)
    g_router = dot_first(normed_two, d_logits)
    d_normed_two = dot_last(d_logits, router_w)
    d_pairs = (
        (weight_pair[:, :, None] * d_output[None]).astype(jnp.bfloat16).reshape(TOP * tok_count, D)
    )
    d_slots = jnp.concatenate([d_pairs, jnp.zeros((1, D), jnp.bfloat16)])[slot_pair].reshape(
        experts, capacity, D
    )
    d_expert_out = lax.all_to_all(d_slots, "expert", split_axis=0, concat_axis=0, tiled=True)
    flat_out = d_expert_out.reshape(experts * capacity, D)
    hidden_flat = hidden_pre.reshape(experts * capacity, HIDDEN_SIZE)
    hidden_act = gelu_tanh(hidden_flat).astype(jnp.bfloat16)
    g_out = dot_first(hidden_act, flat_out)
    d_act = dot_last(flat_out, out_w[0])
    d_pre = jax.vjp(gelu_tanh, hidden_flat)[1](d_act)[0].astype(jnp.bfloat16)
    g_in = dot_first(received.reshape(experts * capacity, D), d_pre)
    d_rows = dot_last(d_pre, in_w[0]).astype(jnp.bfloat16).reshape(experts, capacity, D)
    d_back = lax.all_to_all(d_rows, "expert", split_axis=0, concat_axis=0, tiled=True)
    d_pair_in = jnp.concatenate(
        [d_back.reshape(experts * capacity, D), jnp.zeros((1, D), jnp.bfloat16)]
    )[flat_slot]
    d_pair_in = d_pair_in.astype(jnp.float32).reshape(TOP, tok_count, D)
    d_normed_two = d_normed_two + jnp.sum(d_pair_in, axis=0)
    pulled_two = jax.vjp(layer_norm, middle, norm_scale[1], norm_shift[1])[1](d_normed_two)
    d_middle = d_output + pulled_two[0]
    d_branch = d_middle.astype(jnp.bfloat16)
    g_proj = dot_first(mixed_heads, d_branch)
    d_mixed = dot_last(d_branch, proj_w).astype(jnp.bfloat16).reshape(seq_count, SEQ, HEADS, HEAD)
    query_heads = heads[:, :, 0]
    key_heads = heads[:, :, 1]
    value_heads = heads[:, :, 2]
    scores = (
        jnp.einsum("sqhd,skhd->shqk", query_heads, key_heads, preferred_element_type=jnp.float32)
        * score_scale
    )
    soft_scores = jnp.exp(scores - log_total)
    d_soft = jnp.einsum("sqhd,skhd->shqk", d_mixed, value_heads, preferred_element_type=jnp.float32)
    d_values = jnp.einsum(
        "shqk,sqhd->skhd",
        soft_scores.astype(jnp.bfloat16),
        d_mixed,
        preferred_element_type=jnp.float32,
    )
    d_scores = (
        soft_scores * (d_soft - jnp.sum(soft_scores * d_soft, axis=-1, keepdims=True))
    ).astype(jnp.bfloat16)
    d_query = (
        jnp.einsum("shqk,skhd->sqhd", d_scores, key_heads, preferred_element_type=jnp.float32)
        * score_scale
    )
    d_keys = (
        jnp.einsum("shqk,sqhd->skhd", d_scores, query_heads, preferred_element_type=jnp.float32)
        * score_scale
    )
    d_qkv = (
        jnp.stack([d_query, d_keys, d_values], axis=2)
        .reshape(tok_count, 3 * D)
        .astype(jnp.bfloat16)
    )
    g_qkv = dot_first(normed, d_qkv)
    d_normed = dot_last(d_qkv, qkv_w)
    pulled_one = jax.vjp(layer_norm, residual, norm_scale[0], norm_shift[0])[1](d_normed)
    d_residual = d_middle + pulled_one[0]
    g_gain = jnp.stack([pulled_one[1], pulled_two[1]])
    g_shift = jnp.stack([pulled_one[2], pulled_two[2]])
    return (d_residual, (g_gain, g_shift, g_qkv, g_proj, g_router, g_in[None], g_out[None]))


def local(
    tokens,
    routes,
    priority,
    norm_gain,
    norm_bias,
    w_qkv,
    w_proj,
    w_router,
    exp_in,
    exp_out,
    cotangent,
):
    experts = lax.axis_size("expert") * EXP_DEV
    capacity = max(8, (5 * TOK_MB // (2 * experts) + 7) // 8 * 8)
    totals = []
    for layer_index in range(LAYERS):
        totals.append(None)
    out_blocks = []
    grad_blocks = []
    for micro_index in range(MICRO):
        row_start = micro_index * TOK_MB
        residual = tokens[row_start : row_start + TOK_MB]
        route_ids = routes[row_start : row_start + TOK_MB]
        prio_rank = priority[row_start : row_start + TOK_MB]
        saved_list = []
        for layer_index in range(LAYERS):
            weights = (
                lax.all_gather(norm_gain[layer_index], "shard", axis=1, tiled=True),
                lax.all_gather(norm_bias[layer_index], "shard", axis=1, tiled=True),
                lax.all_gather(w_qkv[layer_index], "shard", axis=0, tiled=True),
                lax.all_gather(w_proj[layer_index], "shard", axis=0, tiled=True),
                lax.all_gather(w_router[layer_index], "shard", axis=0, tiled=True),
                lax.all_gather(exp_in[layer_index], "shard", axis=1, tiled=True),
                lax.all_gather(exp_out[layer_index], "shard", axis=1, tiled=True),
            )
            residual, saved_state = forward_layer(
                residual, route_ids, prio_rank, weights, experts, capacity
            )
            saved_list.append(saved_state)
        out_blocks.append(residual)
        d_residual = cotangent[row_start : row_start + TOK_MB]
        for layer_index in reversed(range(LAYERS)):
            weights = (
                lax.all_gather(norm_gain[layer_index], "shard", axis=1, tiled=True),
                lax.all_gather(norm_bias[layer_index], "shard", axis=1, tiled=True),
                lax.all_gather(w_qkv[layer_index], "shard", axis=0, tiled=True),
                lax.all_gather(w_proj[layer_index], "shard", axis=0, tiled=True),
                lax.all_gather(w_router[layer_index], "shard", axis=0, tiled=True),
                lax.all_gather(exp_in[layer_index], "shard", axis=1, tiled=True),
                lax.all_gather(exp_out[layer_index], "shard", axis=1, tiled=True),
            )
            d_residual, layer_grads = backward_layer(
                d_residual, saved_list[layer_index], weights, experts, capacity
            )
            if totals[layer_index] is None:
                totals[layer_index] = layer_grads
            else:
                totals[layer_index] = tuple(
                    (
                        old_sum + new_term
                        for old_sum, new_term in zip(totals[layer_index], layer_grads)
                    )
                )
        grad_blocks.append(d_residual)
    stacked = tuple(
        (
            jnp.stack([totals[layer_index][kind_index] for layer_index in range(LAYERS)])
            for kind_index in range(7)
        )
    )
    scattered = (
        lax.psum_scatter(
            stacked[0].astype(jnp.bfloat16), "shard", scatter_dimension=2, tiled=True
        ).astype(jnp.float32),
        lax.psum_scatter(
            stacked[1].astype(jnp.bfloat16), "shard", scatter_dimension=2, tiled=True
        ).astype(jnp.float32),
        lax.psum_scatter(
            stacked[2].astype(jnp.bfloat16), "shard", scatter_dimension=1, tiled=True
        ).astype(jnp.float32),
        lax.psum_scatter(
            stacked[3].astype(jnp.bfloat16), "shard", scatter_dimension=1, tiled=True
        ).astype(jnp.float32),
        lax.psum_scatter(
            stacked[4].astype(jnp.bfloat16), "shard", scatter_dimension=1, tiled=True
        ).astype(jnp.float32),
        lax.psum_scatter(
            stacked[5].astype(jnp.bfloat16), "shard", scatter_dimension=2, tiled=True
        ).astype(jnp.float32),
        lax.psum_scatter(
            stacked[6].astype(jnp.bfloat16), "shard", scatter_dimension=2, tiled=True
        ).astype(jnp.float32),
    )
    replicated = (
        lax.psum(scattered[0].astype(jnp.bfloat16), "expert").astype(jnp.float32),
        lax.psum(scattered[1].astype(jnp.bfloat16), "expert").astype(jnp.float32),
        lax.psum(scattered[2].astype(jnp.bfloat16), "expert").astype(jnp.float32),
        lax.psum(scattered[3].astype(jnp.bfloat16), "expert").astype(jnp.float32),
        lax.psum(scattered[4].astype(jnp.bfloat16), "expert").astype(jnp.float32),
    )
    activations = jnp.concatenate(out_blocks, axis=0)
    d_tokens = jnp.concatenate(grad_blocks, axis=0)
    return (
        activations,
        d_tokens,
        replicated[0],
        replicated[1],
        replicated[2],
        replicated[3],
        replicated[4],
        scattered[5],
        scattered[6],
    )


def solution(mesh):
    return jax.shard_map(
        local,
        mesh=mesh,
        in_specs=(
            P(("expert", "shard"), None),
            P(("expert", "shard"), None),
            P(("expert", "shard")),
            P(None, None, "shard"),
            P(None, None, "shard"),
            P(None, "shard", None),
            P(None, "shard", None),
            P(None, "shard", None),
            P(None, "expert", "shard", None),
            P(None, "expert", "shard", None),
            P(("expert", "shard"), None),
        ),
        out_specs=(
            P(("expert", "shard"), None),
            P(("expert", "shard"), None),
            P(None, None, "shard"),
            P(None, None, "shard"),
            P(None, "shard", None),
            P(None, "shard", None),
            P(None, "shard", None),
            P(None, "expert", "shard", None),
            P(None, "expert", "shard", None),
        ),
        check_vma=False,
    )
```

profile of v0, /device:TPU:0, one launch (start us, length us, event | category | flops | bytes accessed | tf_op | source)
XLA Modules:
  0.0 1039.3 jit_solution(6262433277946074067)
XLA Ops:
  26.5 8.2 all-gather.3
  116.0 8.7 all-to-all-done.4
  163.2 8.9 multiply_convert_fusion.3
  177.4 12.0 %all-to-all-done.5 = bf16[8,128,512]{2,1,0:T(8,128)(2,1)} async-done(((bf16[8,128,512]{2,1,0:T(8,128)(2,1)}), bf16[8,128,512]{2,1,0:T(8,128)(2,1)}, u32[]{:S(2)}, u32[]{:S(2)}) %all-to-all-start.5) | async-done | bytes 1048608 | tf_op jit(solution)/shard_map/all_to_all | solution.py:106
  207.8 11.5 %all-to-all-done.1 = bf16[8,128,512]{2,1,0:T(8,128)(2,1)} async-done(((bf16[8,128,512]{2,1,0:T(8,128)(2,1)}), bf16[8,128,512]{2,1,0:T(8,128)(2,1)}, u32[]{:S(2)}, u32[]{:S(2)}) %all-to-all-start.1) | async-done | bytes 1048608 | tf_op jit(solution)/shard_map/all_to_all | solution.py:106
  315.1 18.7 %all-to-all-done.8 = bf16[8,128,512]{2,1,0:T(8,128)(2,1)} async-done(((bf16[8,128,512]{2,1,0:T(8,128)(2,1)}), bf16[8,128,512]{2,1,0:T(8,128)(2,1)}, u32[]{:S(2)}, u32[]{:S(2)}) %all-to-all-start.8) | async-done | bytes 1048608 | tf_op jit(solution)/shard_map/all_to_all | solution.py:189
  349.9 13.5 %all-to-all-done.6 = bf16[8,128,512]{2,1,0:T(8,128)(2,1)} async-done(((bf16[8,128,512]{2,1,0:T(8,128)(2,1)}), bf16[8,128,512]{2,1,0:T(8,128)(2,1)}, u32[]{:S(2)}, u32[]{:S(2)}) %all-to-all-start.6) | async-done | bytes 1048608 | tf_op jit(solution)/shard_map/all_to_all | solution.py:97
  368.7 9.9 multiply_convert_fusion.2
  384.8 8.3 all-to-all-done.12
  397.7 9.7 fusion.13
  412.7 11.0 %all-to-all-done.3 = bf16[8,128,512]{2,1,0:T(8,128)(2,1)S(1)} async-done(((bf16[8,128,512]{2,1,0:T(8,128)(2,1)}), bf16[8,128,512]{2,1,0:T(8,128)(2,1)S(1)}, u32[]{:S(2)}, u32[]{:S(2)}) %all-to-all-start.3) | async-done | bytes 1048608 | tf_op jit(solution)/shard_map/all_to_all | solution.py:106
  443.6 10.1 all-to-all-done.9
  457.3 9.7 fusion.27
  472.3 10.8 %all-to-all-done.7 = bf16[8,128,512]{2,1,0:T(8,128)(2,1)S(1)} async-done(((bf16[8,128,512]{2,1,0:T(8,128)(2,1)}), bf16[8,128,512]{2,1,0:T(8,128)(2,1)S(1)}, u32[]{:S(2)}, u32[]{:S(2)}) %all-to-all-start.7) | async-done | bytes 1048608 | tf_op jit(solution)/shard_map/all_to_all | solution.py:106
  621.2 9.7 fusion.6
  636.4 10.6 %all-to-all-done.14 = bf16[8,128,512]{2,1,0:T(8,128)(2,1)S(1)} async-done(((bf16[8,128,512]{2,1,0:T(8,128)(2,1)}), bf16[8,128,512]{2,1,0:T(8,128)(2,1)S(1)}, u32[]{:S(2)}, u32[]{:S(2)}) %all-to-all-start.14) | async-done | bytes 1048608 | tf_op jit(solution)/shard_map/all_to_all | solution.py:189
  651.6 9.7 fusion.20
  666.6 11.0 %all-to-all-done.11 = bf16[8,128,512]{2,1,0:T(8,128)(2,1)S(1)} async-done(((bf16[8,128,512]{2,1,0:T(8,128)(2,1)}), bf16[8,128,512]{2,1,0:T(8,128)(2,1)S(1)}, u32[]{:S(2)}, u32[]{:S(2)}) %all-to-all-start.11) | async-done | bytes 1048608 | tf_op jit(solution)/shard_map/all_to_all | solution.py:198
  776.2 9.7 fusion.39
  834.6 17.8 %reduce-scatter.22.cloned.1.call-done = bf16[128,4]{1,0:T(8,128)(2,1)} async-done(((bf16[512,4]{1,0:T(8,128)(2,1)}), bf16[128,4]{1,0:T(8,128)(2,1)}) %reduce-scatter.22.cloned.1.call-update) | async-done | bytes 1040
  853.3 21.6 %all-reduce.16 = (bf16[2,2,128]{2,1,0:T(2,128)(2,1)S(1)}, bf16[2,2,128]{2,1,0:T(2,128)(2,1)S(1)}, bf16[2,128,8]{1,2,0:T(8,128)(2,1)S(1)}) all-reduce(bf16[2,2,128]{2,1,0:T(2,128)(2,1)S(1)} %copy.259, bf16[2,2,128]{2,1,0:T(2,128)(2,1)S(1)} %copy.261, bf16[2,128,8]{1,2,0:T(8,128)(2,1)S(1)} %copy.263), channel_id=1, replica_groups=mesh['expert'=8,'shard'=4] {'expert'}, use_global_device_ids=true, to_apply=%region_89.90 | all-reduce | flops 3072 | bytes 12288 | tf_op jit(solution)/shard_map/psum | solution.py:344
  876.7 22.7 %reduce-scatter.20.cloned.1.call-done = bf16[2,1,512,512]{3,2,1,0:T(8,128)(2,1)} async-done(((bf16[2,1,2048,512]{3,2,1,0:T(8,128)(2,1)}), bf16[2,1,512,512]{3,2,1,0:T(8,128)(2,1)}) %reduce-scatter.20.cloned.1.call-update) | async-done | bytes 1048592 | tf_op jit(solution)/shard_map/reduce_scatter | solution.py:339
  902.3 44.3 %reduce-scatter.18.cloned.1.call-done = bf16[2,1,128,2048]{3,2,1,0:T(8,128)(2,1)} async-done(((bf16[2,1,512,2048]{3,2,1,0:T(8,128)(2,1)}), bf16[2,1,128,2048]{3,2,1,0:T(8,128)(2,1)}) %reduce-scatter.18.cloned.1.call-update) | async-done | bytes 1048592 | tf_op jit(solution)/shard_map/reduce_scatter | solution.py:336
  949.3 79.0 %all-reduce.20.cloned.1.call-done = (bf16[2,128,1536]{2,1,0:T(8,128)(2,1)}, bf16[2,128,512]{2,1,0:T(8,128)(2,1)}) async-done(((bf16[2,128,1536]{2,1,0:T(8,128)(2,1)}, bf16[2,128,512]{2,1,0:T(8,128)(2,1)}), (bf16[2,128,1536]{2,1,0:T(8,128)(2,1)}, bf16[2,128,512]{2,1,0:T(8,128)(2,1)})) %all-reduce.20.cloned.1.call-update) | async-done | bytes 1048592 | tf_op jit(solution)/shard_map/psum | solution.py:346
  (987 shorter events, 634.3 us)
Async XLA Ops:
  7.2 34.5 %all-gather.21.cloned.1.call-start = ((), (), s32[]{:S(2)}) async-start(), calls=%async_computation.27 | async-start | bytes 1966080 | tf_op jit(solution)/shard_map/all_gather | solution.py:279
  9.5 132.4 %all-gather.23.cloned.1.call-start = ((), (), s32[]{:S(2)}) async-start(), calls=%async_computation.28 | async-start | bytes 2621440 | tf_op jit(solution)/shard_map/all_gather | solution.py:282
  11.8 137.6 %all-gather.25.cloned.1.call-start = ((), (), s32[]{:S(2)}) async-start(), calls=%async_computation.29 | async-start | bytes 2621440 | tf_op jit(solution)/shard_map/all_gather | solution.py:283
  92.8 31.9 %all-to-all-start.4 = ((bf16[8,128,512]{2,1,0:T(8,128)(2,1)}), bf16[8,128,512]{2,1,0:T(8,128)(2,1)}, u32[]{:S(2)}, u32[]{:S(2)}) async-start(bf16[8,128,512]{2,1,0:T(8,128)(2,1)} %bitcast.478), calls=%async_computation.4 | async-start | bytes 2097152 | tf_op jit(solution)/shard_map/all_to_all | solution.py:97
  98.4 132.7 %all-gather.27.cloned.1.call-start = ((), (), s32[]{:S(2)}) async-start(), calls=%async_computation.30 | async-start | bytes 1966080 | tf_op jit(solution)/shard_map/all_gather | solution.py:279
  124.7 32.4 %all-to-all-start = ((bf16[8,128,512]{2,1,0:T(8,128)(2,1)}), bf16[8,128,512]{2,1,0:T(8,128)(2,1)}, u32[]{:S(2)}, u32[]{:S(2)}) async-start(bf16[8,128,512]{2,1,0:T(8,128)(2,1)} %bitcast.482), calls=%async_computation | async-start | bytes 2097152 | tf_op jit(solution)/shard_map/all_to_all | solution.py:97
  157.2 32.3 %all-to-all-start.5 = ((bf16[8,128,512]{2,1,0:T(8,128)(2,1)}), bf16[8,128,512]{2,1,0:T(8,128)(2,1)}, u32[]{:S(2)}, u32[]{:S(2)}) async-start(bf16[8,128,512]{2,1,0:T(8,128)(2,1)} %bitcast.496), calls=%async_computation.5 | async-start | bytes 2097152 | tf_op jit(solution)/shard_map/all_to_all | solution.py:106
  189.4 29.8 %all-to-all-start.1 = ((bf16[8,128,512]{2,1,0:T(8,128)(2,1)}), bf16[8,128,512]{2,1,0:T(8,128)(2,1)}, u32[]{:S(2)}, u32[]{:S(2)}) async-start(bf16[8,128,512]{2,1,0:T(8,128)(2,1)} %bitcast.494), calls=%async_computation.1 | async-start | bytes 2097152 | tf_op jit(solution)/shard_map/all_to_all | solution.py:106
  274.4 29.7 %all-to-all-start.2 = ((bf16[8,128,512]{2,1,0:T(8,128)(2,1)}), bf16[8,128,512]{2,1,0:T(8,128)(2,1)}, u32[]{:S(2)}, u32[]{:S(2)}) async-start(bf16[8,128,512]{2,1,0:T(8,128)(2,1)} %bitcast.480), calls=%async_computation.2 | async-start | bytes 2097152 | tf_op jit(solution)/shard_map/all_to_all | solution.py:97
  278.6 90.1 %all-gather.29.cloned.1.call-start = ((), (), s32[]{:S(2)}) async-start(), calls=%async_computation.31 | async-start | bytes 2621440 | tf_op jit(solution)/shard_map/all_gather | solution.py:282
  308.3 70.3 %all-gather.31.cloned.1.call-start = ((), (), s32[]{:S(2)}) async-start(), calls=%async_computation.32 | async-start | bytes 2621440 | tf_op jit(solution)/shard_map/all_gather | solution.py:283
  363.4 29.7 %all-to-all-start.12 = ((bf16[8,128,512]{2,1,0:T(8,128)(2,1)}), bf16[8,128,512]{2,1,0:T(8,128)(2,1)S(1)}, u32[]{:S(2)}, u32[]{:S(2)}) async-start(bf16[8,128,512]{2,1,0:T(8,128)(2,1)} %bitcast.484), calls=%async_computation.12 | async-start | bytes 2097152 | tf_op jit(solution)/shard_map/all_to_all | solution.py:189
  423.7 30.0 %all-to-all-start.9 = ((bf16[8,128,512]{2,1,0:T(8,128)(2,1)}), bf16[8,128,512]{2,1,0:T(8,128)(2,1)}, u32[]{:S(2)}, u32[]{:S(2)}) async-start(bf16[8,128,512]{2,1,0:T(8,128)(2,1)} %bitcast.495), calls=%async_computation.9 | async-start | bytes 2097152 | tf_op jit(solution)/shard_map/all_to_all | solution.py:198
  483.1 34.0 %all-to-all-start.13 = ((bf16[8,128,512]{2,1,0:T(8,128)(2,1)}), bf16[8,128,512]{2,1,0:T(8,128)(2,1)}, u32[]{:S(2)}, u32[]{:S(2)}) async-start(bf16[8,128,512]{2,1,0:T(8,128)(2,1)} %bitcast.493), calls=%async_computation.13 | async-start | bytes 2097152 | tf_op jit(solution)/shard_map/all_to_all | solution.py:198
  586.3 31.2 %all-to-all-start.10 = ((bf16[8,128,512]{2,1,0:T(8,128)(2,1)}), bf16[8,128,512]{2,1,0:T(8,128)(2,1)}, u32[]{:S(2)}, u32[]{:S(2)}) async-start(bf16[8,128,512]{2,1,0:T(8,128)(2,1)} %bitcast.477), calls=%async_computation.10 | async-start | bytes 2097152 | tf_op jit(solution)/shard_map/all_to_all | solution.py:189
  678.5 30.0 %all-to-all-start.15 = ((bf16[8,128,512]{2,1,0:T(8,128)(2,1)}), bf16[8,128,512]{2,1,0:T(8,128)(2,1)}, u32[]{:S(2)}, u32[]{:S(2)}) async-start(bf16[8,128,512]{2,1,0:T(8,128)(2,1)} %bitcast.492), calls=%async_computation.15 | async-start | bytes 2097152 | tf_op jit(solution)/shard_map/all_to_all | solution.py:198
  682.9 143.7 %reduce-scatter.26.cloned.1.call-start = ((), (), s32[]{:S(2)}) async-start(), calls=%async_computation.35 | async-start | bytes 163840
  688.8 142.0 %reduce-scatter.16.cloned.1.call-start = ((), (), s32[]{:S(2)}) async-start(), calls=%async_computation.24 | async-start | bytes 1310720 | tf_op jit(solution)/shard_map/reduce_scatter | solution.py:330
  744.1 86.7 %reduce-scatter.14.cloned.1.call-start = ((), (), s32[]{:S(2)}) async-start(), calls=%async_computation.23 | async-start | bytes 3932160 | tf_op jit(solution)/shard_map/reduce_scatter | solution.py:327
  770.7 63.0 %reduce-scatter.24.cloned.1.call-start = ((), (), s32[]{:S(2)}) async-start(), calls=%async_computation.34 | async-start | bytes 163840
  799.1 53.3 %reduce-scatter.22.cloned.1.call-start = ((), (), s32[]{:S(2)}) async-start(), calls=%async_computation.33 | async-start | bytes 163840
  800.4 99.0 %reduce-scatter.20.cloned.1.call-start = ((), (), s32[]{:S(2)}) async-start(), calls=%async_computation.26 | async-start | bytes 5242880 | tf_op jit(solution)/shard_map/reduce_scatter | solution.py:339
  805.1 141.4 %reduce-scatter.18.cloned.1.call-start = ((), (), s32[]{:S(2)}) async-start(), calls=%async_computation.25 | async-start | bytes 5242880 | tf_op jit(solution)/shard_map/reduce_scatter | solution.py:336
  823.9 204.4 %all-reduce.20.cloned.1.call-start = ((), (), s32[]{:S(2)}) async-start(), calls=%async_computation.36 | async-start | bytes 2097152 | tf_op jit(solution)/shard_map/psum | solution.py:346
  (288 other events, 3266.5 us)
Sparse Core Ops, SparseCore 0:
  10.1 23.2 all-gather.20
  35.6 21.9 all-gather.22
  59.8 22.5 all-gather.24
  100.4 20.5 all-gather.26
  280.7 23.2 all-gather.28
  310.4 23.2 all-gather.30
  688.9 20.3 reduce-scatter.25
  744.2 23.0 reduce-scatter.15
  770.9 36.8 reduce-scatter.13
  810.1 19.6 reduce-scatter.23
  832.7 19.6 reduce-scatter.21
  854.8 44.5 reduce-scatter.19
  901.9 44.5 reduce-scatter.17
  949.9 78.2 all-reduce.19
where the time goes:
time: 1050 us; the launch traced here: 1040 us
  waiting for transfers between devices  311 us (30%)
  local copies, waits for them, and re-layouts  258 us (25%)
  matrix products  229 us (22%)
  other arithmetic  82.1 us (8%)
  starting transfers between devices  71.9 us (7%)
  blocking collectives  69.1 us (7%)
  between operations  18.1 us (2%)
    psum x1, waiting for transfers between devices, local(): lax.psum(scattered[2].astype(jnp.bfloat16), 'expert').astype(jnp.float32)  79 us
    dot_general x20, matrix products, dot_last(): lax.dot_general(left, right, (((1,), (1,)), ((), ())), preferred_element_...  70.6 us
    dot_general x20, matrix products, dot_first(): lax.dot_general(left, right, (((0,), (0,)), ((), ())), preferred_element_...  57.3 us
    unnamed x588, local copies, waits for them, and re-layouts  53.8 us
    all_to_all x4, waiting for transfers between devices, forward_layer(): lax.all_to_all(expert_rows.reshape(sources, item_count, D), 'expert', spl...  45.3 us
    all_to_all x4, waiting for transfers between devices, backward_layer(): lax.all_to_all(d_slots, 'expert', split_axis=0, concat_axis=0, tiled=True)  45 us
    reduce_scatter x1, waiting for transfers between devices, local(): lax.psum_scatter(stacked[5].astype(jnp.bfloat16), 'shard', scatter_dimens...  44.3 us
    dot_general x4, matrix products, forward_layer(): hidden_pre = jnp.dot(row_block, in_w[0], preferred_element_type=jnp.float32)  30.8 us
  transfers between devices with their start and end apart: 30, of which 18 were waited for; matrix products, arithmetic and copies ran while one was open for 41% of the time, Pallas kernels for 0%

commit v1 on v0

--- a/solution.py
+++ b/solution.py
@@ -1,3 +1,4 @@
+import functools
 import jax
 import jax.numpy as jnp
 from jax import lax
@@ -14,6 +15,14 @@
 TOP = 2
 TOK_MB = 394
 norm_eps = 1e-06
+
+
+def shape_group_all(xx, axis_key):
+    part_now = jnp.sum(jax.lax.all_gather(xx, axis_key), 0)
+    return part_now
+
+
+move_windows = functools.partial(shape_group_all, axis_key="expert")
 
 
 def layer_norm(values, norm_scale, norm_shift):
@@ -341,7 +350,7 @@
         ).astype(jnp.float32),
     )
     replicated = (
-        lax.psum(scattered[0].astype(jnp.bfloat16), "expert").astype(jnp.float32),
+        move_windows(scattered[0].astype(jnp.bfloat16)).astype(jnp.float32),
         lax.psum(scattered[1].astype(jnp.bfloat16), "expert").astype(jnp.float32),
         lax.psum(scattered[2].astype(jnp.bfloat16), "expert").astype(jnp.float32),
         lax.psum(scattered[3].astype(jnp.bfloat16), "expert").astype(jnp.float32),

time: 1050 us -> 1050 us (level)
  blocking collectives: 69.1 us -> 84.6 us
  waiting for transfers between devices: 311 us -> 296 us
    unnamed x17, waiting for transfers between devices: 19.5 us -> 1.76 us
    all_gather x0 -> x1, blocking collectives: none -> 17.6 us  [shape_group_all(): part_now = jnp.sum(jax.lax.all_gather(xx, axis_key), 0)]
  transfers between devices with their start and end apart: 30 -> 30, of which waited for: 18 -> 17; matrix products, arithmetic and copies ran while one was open for 41% -> 41% of each run, Pallas kernels for 0% -> 0%
where the time goes in v1:
time: 1050 us; the launch traced here: 1040 us
  waiting for transfers between devices  296 us (28%)
  local copies, waits for them, and re-layouts  258 us (25%)
  matrix products  229 us (22%)
  blocking collectives  84.6 us (8%)
  other arithmetic  82.1 us (8%)
  starting transfers between devices  71.9 us (7%)
  between operations  18.1 us (2%)
    psum x1, waiting for transfers between devices, local(): lax.psum(scattered[2].astype(jnp.bfloat16), 'expert').astype(jnp.float32)  79 us
    dot_general x20, matrix products, dot_last(): lax.dot_general(left, right, (((1,), (1,)), ((), ())), preferred_element_...  70.6 us
    dot_general x20, matrix products, dot_first(): lax.dot_general(left, right, (((0,), (0,)), ((), ())), preferred_element_...  57.3 us
    unnamed x588, local copies, waits for them, and re-layouts  53.8 us
    all_to_all x4, waiting for transfers between devices, forward_layer(): lax.all_to_all(expert_rows.reshape(sources, item_count, D), 'expert', spl...  45.3 us
    all_to_all x4, waiting for transfers between devices, backward_layer(): lax.all_to_all(d_slots, 'expert', split_axis=0, concat_axis=0, tiled=True)  45 us
    reduce_scatter x1, waiting for transfers between devices, local(): lax.psum_scatter(stacked[5].astype(jnp.bfloat16), 'shard', scatter_dimens...  44.3 us
    dot_general x4, matrix products, forward_layer(): hidden_pre = jnp.dot(row_block, in_w[0], preferred_element_type=jnp.float32)  30.7 us
  transfers between devices with their start and end apart: 30, of which 17 were waited for; matrix products, arithmetic and copies ran while one was open for 41% of the time, Pallas kernels for 0%

profile of v1, /device:TPU:0, one launch (start us, length us, event | category | flops | bytes accessed | tf_op | source)
XLA Modules:
  0.0 1039.4 jit_solution(13648900708640493041)
XLA Ops:
  26.5 8.2 all-gather.3
  116.0 8.8 all-to-all-done.4
  163.1 8.9 multiply_convert_fusion.3
  177.4 12.0 %all-to-all-done.5 = bf16[8,128,512]{2,1,0:T(8,128)(2,1)} async-done(((bf16[8,128,512]{2,1,0:T(8,128)(2,1)}), bf16[8,128,512]{2,1,0:T(8,128)(2,1)}, u32[]{:S(2)}, u32[]{:S(2)}) %all-to-all-start.5) | async-done | bytes 1048608 | tf_op jit(solution)/shard_map/all_to_all | solution.py:115
  207.8 11.5 %all-to-all-done.1 = bf16[8,128,512]{2,1,0:T(8,128)(2,1)} async-done(((bf16[8,128,512]{2,1,0:T(8,128)(2,1)}), bf16[8,128,512]{2,1,0:T(8,128)(2,1)}, u32[]{:S(2)}, u32[]{:S(2)}) %all-to-all-start.1) | async-done | bytes 1048608 | tf_op jit(solution)/shard_map/all_to_all | solution.py:115
  315.1 18.7 %all-to-all-done.8 = bf16[8,128,512]{2,1,0:T(8,128)(2,1)} async-done(((bf16[8,128,512]{2,1,0:T(8,128)(2,1)}), bf16[8,128,512]{2,1,0:T(8,128)(2,1)}, u32[]{:S(2)}, u32[]{:S(2)}) %all-to-all-start.8) | async-done | bytes 1048608 | tf_op jit(solution)/shard_map/all_to_all | solution.py:198
  350.0 13.5 %all-to-all-done.6 = bf16[8,128,512]{2,1,0:T(8,128)(2,1)} async-done(((bf16[8,128,512]{2,1,0:T(8,128)(2,1)}), bf16[8,128,512]{2,1,0:T(8,128)(2,1)}, u32[]{:S(2)}, u32[]{:S(2)}) %all-to-all-start.6) | async-done | bytes 1048608 | tf_op jit(solution)/shard_map/all_to_all | solution.py:106
  368.7 9.9 multiply_convert_fusion.2
  384.8 8.4 all-to-all-done.12
  397.8 9.7 fusion.13
  412.8 11.0 %all-to-all-done.3 = bf16[8,128,512]{2,1,0:T(8,128)(2,1)S(1)} async-done(((bf16[8,128,512]{2,1,0:T(8,128)(2,1)}), bf16[8,128,512]{2,1,0:T(8,128)(2,1)S(1)}, u32[]{:S(2)}, u32[]{:S(2)}) %all-to-all-start.3) | async-done | bytes 1048608 | tf_op jit(solution)/shard_map/all_to_all | solution.py:115
  443.7 10.1 all-to-all-done.9
  457.3 9.7 fusion.27
  472.3 10.8 %all-to-all-done.7 = bf16[8,128,512]{2,1,0:T(8,128)(2,1)S(1)} async-done(((bf16[8,128,512]{2,1,0:T(8,128)(2,1)}), bf16[8,128,512]{2,1,0:T(8,128)(2,1)S(1)}, u32[]{:S(2)}, u32[]{:S(2)}) %all-to-all-start.7) | async-done | bytes 1048608 | tf_op jit(solution)/shard_map/all_to_all | solution.py:115
  621.3 9.7 fusion.6
  636.4 10.6 %all-to-all-done.14 = bf16[8,128,512]{2,1,0:T(8,128)(2,1)S(1)} async-done(((bf16[8,128,512]{2,1,0:T(8,128)(2,1)}), bf16[8,128,512]{2,1,0:T(8,128)(2,1)S(1)}, u32[]{:S(2)}, u32[]{:S(2)}) %all-to-all-start.14) | async-done | bytes 1048608 | tf_op jit(solution)/shard_map/all_to_all | solution.py:198
  651.7 9.7 fusion.20
  666.6 11.0 %all-to-all-done.11 = bf16[8,128,512]{2,1,0:T(8,128)(2,1)S(1)} async-done(((bf16[8,128,512]{2,1,0:T(8,128)(2,1)}), bf16[8,128,512]{2,1,0:T(8,128)(2,1)S(1)}, u32[]{:S(2)}, u32[]{:S(2)}) %all-to-all-start.11) | async-done | bytes 1048608 | tf_op jit(solution)/shard_map/all_to_all | solution.py:207
  776.3 9.7 fusion.39
  834.7 19.5 %all-reduce.16 = (bf16[2,2,128]{2,1,0:T(2,128)(2,1)S(1)}, bf16[2,128,8]{1,2,0:T(8,128)(2,1)S(1)}) all-reduce(bf16[2,2,128]{2,1,0:T(2,128)(2,1)S(1)} %copy.261, bf16[2,128,8]{1,2,0:T(8,128)(2,1)S(1)} %copy.263), channel_id=1, replica_groups=mesh['expert'=8,'shard'=4] {'expert'}, use_global_device_ids=true, to_apply=%region_99.100 | all-reduce | flops 2560 | bytes 10240 | tf_op jit(solution)/shard_map/psum | solution.py:354
  856.4 17.6 %all-gather.14 = bf16[16,2,128]{2,1,0:T(2,128)(2,1)S(1)} all-gather(bf16[2,2,128]{2,1,0:T(2,128)(2,1)S(1)} %copy.259), channel_id=16, replica_groups=mesh['expert'=8,'shard'=4] {'expert'}, dimensions={0}, use_global_device_ids=true | all-gather | bytes 9216 | tf_op jit(solution)/shard_map/all_gather | solution.py:21
  874.6 24.9 %reduce-scatter.20.cloned.1.call-done = bf16[2,1,512,512]{3,2,1,0:T(8,128)(2,1)} async-done(((bf16[2,1,2048,512]{3,2,1,0:T(8,128)(2,1)}), bf16[2,1,512,512]{3,2,1,0:T(8,128)(2,1)}) %reduce-scatter.20.cloned.1.call-update) | async-done | bytes 1048592 | tf_op jit(solution)/shard_map/reduce_scatter | solution.py:348
  902.3 44.3 %reduce-scatter.18.cloned.1.call-done = bf16[2,1,128,2048]{3,2,1,0:T(8,128)(2,1)} async-done(((bf16[2,1,512,2048]{3,2,1,0:T(8,128)(2,1)}), bf16[2,1,128,2048]{3,2,1,0:T(8,128)(2,1)}) %reduce-scatter.18.cloned.1.call-update) | async-done | bytes 1048592 | tf_op jit(solution)/shard_map/reduce_scatter | solution.py:345
  949.4 79.0 %all-reduce.20.cloned.1.call-done = (bf16[2,128,1536]{2,1,0:T(8,128)(2,1)}, bf16[2,128,512]{2,1,0:T(8,128)(2,1)}) async-done(((bf16[2,128,1536]{2,1,0:T(8,128)(2,1)}, bf16[2,128,512]{2,1,0:T(8,128)(2,1)}), (bf16[2,128,1536]{2,1,0:T(8,128)(2,1)}, bf16[2,128,512]{2,1,0:T(8,128)(2,1)})) %all-reduce.20.cloned.1.call-update) | async-done | bytes 1048592 | tf_op jit(solution)/shard_map/psum | solution.py:355
  (989 shorter events, 634.3 us)
Async XLA Ops:
  7.2 34.5 %all-gather.22.cloned.1.call-start = ((), (), s32[]{:S(2)}) async-start(), calls=%async_computation.27 | async-start | bytes 1966080 | tf_op jit(solution)/shard_map/all_gather | solution.py:288
  9.5 132.4 %all-gather.24.cloned.1.call-start = ((), (), s32[]{:S(2)}) async-start(), calls=%async_computation.28 | async-start | bytes 2621440 | tf_op jit(solution)/shard_map/all_gather | solution.py:291
  11.8 137.6 %all-gather.26.cloned.1.call-start = ((), (), s32[]{:S(2)}) async-start(), calls=%async_computation.29 | async-start | bytes 2621440 | tf_op jit(solution)/shard_map/all_gather | solution.py:292
  92.8 31.9 %all-to-all-start.4 = ((bf16[8,128,512]{2,1,0:T(8,128)(2,1)}), bf16[8,128,512]{2,1,0:T(8,128)(2,1)}, u32[]{:S(2)}, u32[]{:S(2)}) async-start(bf16[8,128,512]{2,1,0:T(8,128)(2,1)} %bitcast.479), calls=%async_computation.4 | async-start | bytes 2097152 | tf_op jit(solution)/shard_map/all_to_all | solution.py:106
  98.3 132.8 %all-gather.28.cloned.1.call-start = ((), (), s32[]{:S(2)}) async-start(), calls=%async_computation.30 | async-start | bytes 1966080 | tf_op jit(solution)/shard_map/all_gather | solution.py:288
  124.7 32.4 %all-to-all-start = ((bf16[8,128,512]{2,1,0:T(8,128)(2,1)}), bf16[8,128,512]{2,1,0:T(8,128)(2,1)}, u32[]{:S(2)}, u32[]{:S(2)}) async-start(bf16[8,128,512]{2,1,0:T(8,128)(2,1)} %bitcast.483), calls=%async_computation | async-start | bytes 2097152 | tf_op jit(solution)/shard_map/all_to_all | solution.py:106
  157.2 32.3 %all-to-all-start.5 = ((bf16[8,128,512]{2,1,0:T(8,128)(2,1)}), bf16[8,128,512]{2,1,0:T(8,128)(2,1)}, u32[]{:S(2)}, u32[]{:S(2)}) async-start(bf16[8,128,512]{2,1,0:T(8,128)(2,1)} %bitcast.497), calls=%async_computation.5 | async-start | bytes 2097152 | tf_op jit(solution)/shard_map/all_to_all | solution.py:115
  189.4 29.9 %all-to-all-start.1 = ((bf16[8,128,512]{2,1,0:T(8,128)(2,1)}), bf16[8,128,512]{2,1,0:T(8,128)(2,1)}, u32[]{:S(2)}, u32[]{:S(2)}) async-start(bf16[8,128,512]{2,1,0:T(8,128)(2,1)} %bitcast.495), calls=%async_computation.1 | async-start | bytes 2097152 | tf_op jit(solution)/shard_map/all_to_all | solution.py:115
  274.4 29.7 %all-to-all-start.2 = ((bf16[8,128,512]{2,1,0:T(8,128)(2,1)}), bf16[8,128,512]{2,1,0:T(8,128)(2,1)}, u32[]{:S(2)}, u32[]{:S(2)}) async-start(bf16[8,128,512]{2,1,0:T(8,128)(2,1)} %bitcast.481), calls=%async_computation.2 | async-start | bytes 2097152 | tf_op jit(solution)/shard_map/all_to_all | solution.py:106
  278.7 90.1 %all-gather.30.cloned.1.call-start = ((), (), s32[]{:S(2)}) async-start(), calls=%async_computation.31 | async-start | bytes 2621440 | tf_op jit(solution)/shard_map/all_gather | solution.py:291
  308.4 70.2 %all-gather.32.cloned.1.call-start = ((), (), s32[]{:S(2)}) async-start(), calls=%async_computation.32 | async-start | bytes 2621440 | tf_op jit(solution)/shard_map/all_gather | solution.py:292
  363.4 29.7 %all-to-all-start.12 = ((bf16[8,128,512]{2,1,0:T(8,128)(2,1)}), bf16[8,128,512]{2,1,0:T(8,128)(2,1)S(1)}, u32[]{:S(2)}, u32[]{:S(2)}) async-start(bf16[8,128,512]{2,1,0:T(8,128)(2,1)} %bitcast.485), calls=%async_computation.12 | async-start | bytes 2097152 | tf_op jit(solution)/shard_map/all_to_all | solution.py:198
  423.7 30.0 %all-to-all-start.9 = ((bf16[8,128,512]{2,1,0:T(8,128)(2,1)}), bf16[8,128,512]{2,1,0:T(8,128)(2,1)}, u32[]{:S(2)}, u32[]{:S(2)}) async-start(bf16[8,128,512]{2,1,0:T(8,128)(2,1)} %bitcast.496), calls=%async_computation.9 | async-start | bytes 2097152 | tf_op jit(solution)/shard_map/all_to_all | solution.py:207
  483.1 34.0 %all-to-all-start.13 = ((bf16[8,128,512]{2,1,0:T(8,128)(2,1)}), bf16[8,128,512]{2,1,0:T(8,128)(2,1)}, u32[]{:S(2)}, u32[]{:S(2)}) async-start(bf16[8,128,512]{2,1,0:T(8,128)(2,1)} %bitcast.494), calls=%async_computation.13 | async-start | bytes 2097152 | tf_op jit(solution)/shard_map/all_to_all | solution.py:207
  586.4 31.1 %all-to-all-start.10 = ((bf16[8,128,512]{2,1,0:T(8,128)(2,1)}), bf16[8,128,512]{2,1,0:T(8,128)(2,1)}, u32[]{:S(2)}, u32[]{:S(2)}) async-start(bf16[8,128,512]{2,1,0:T(8,128)(2,1)} %bitcast.478), calls=%async_computation.10 | async-start | bytes 2097152 | tf_op jit(solution)/shard_map/all_to_all | solution.py:198
  678.6 30.0 %all-to-all-start.15 = ((bf16[8,128,512]{2,1,0:T(8,128)(2,1)}), bf16[8,128,512]{2,1,0:T(8,128)(2,1)}, u32[]{:S(2)}, u32[]{:S(2)}) async-start(bf16[8,128,512]{2,1,0:T(8,128)(2,1)} %bitcast.493), calls=%async_computation.15 | async-start | bytes 2097152 | tf_op jit(solution)/shard_map/all_to_all | solution.py:207
  682.9 143.7 %reduce-scatter.26.cloned.1.call-start = ((), (), s32[]{:S(2)}) async-start(), calls=%async_computation.35 | async-start | bytes 163840
  688.8 142.0 %reduce-scatter.16.cloned.1.call-start = ((), (), s32[]{:S(2)}) async-start(), calls=%async_computation.24 | async-start | bytes 1310720 | tf_op jit(solution)/shard_map/reduce_scatter | solution.py:339
  744.1 86.7 %reduce-scatter.14.cloned.1.call-start = ((), (), s32[]{:S(2)}) async-start(), calls=%async_computation.23 | async-start | bytes 3932160 | tf_op jit(solution)/shard_map/reduce_scatter | solution.py:336
  770.8 63.0 %reduce-scatter.24.cloned.1.call-start = ((), (), s32[]{:S(2)}) async-start(), calls=%async_computation.34 | async-start | bytes 163840
  799.2 56.3 %reduce-scatter.22.cloned.1.call-start = ((), (), s32[]{:S(2)}) async-start(), calls=%async_computation.33 | async-start | bytes 163840
  800.5 99.0 %reduce-scatter.20.cloned.1.call-start = ((), (), s32[]{:S(2)}) async-start(), calls=%async_computation.26 | async-start | bytes 5242880 | tf_op jit(solution)/shard_map/reduce_scatter | solution.py:348
  805.2 141.4 %reduce-scatter.18.cloned.1.call-start = ((), (), s32[]{:S(2)}) async-start(), calls=%async_computation.25 | async-start | bytes 5242880 | tf_op jit(solution)/shard_map/reduce_scatter | solution.py:345
  823.9 204.5 %all-reduce.20.cloned.1.call-start = ((), (), s32[]{:S(2)}) async-start(), calls=%async_computation.36 | async-start | bytes 2097152 | tf_op jit(solution)/shard_map/psum | solution.py:355
  (288 other events, 3266.5 us)
Sparse Core Ops, SparseCore 0:
  10.1 23.2 all-gather.21
  35.6 21.9 all-gather.23
  59.8 22.5 all-gather.25
  100.4 20.5 all-gather.27
  280.7 23.3 all-gather.29
  310.4 23.2 all-gather.31
  689.0 20.3 reduce-scatter.25
  744.3 23.0 reduce-scatter.15
  770.9 36.8 reduce-scatter.13
  810.1 19.6 reduce-scatter.23
  832.8 19.6 reduce-scatter.21
  854.9 44.5 reduce-scatter.19
  902.0 44.5 reduce-scatter.17
  950.0 78.3 all-reduce.19
